TPU v7x, 32 devices: a whole 2x2x4 slice. The times are simulated.
32 devices in a mesh: groups: 2 (over y), tm: 4 (over z), comp: 2 (over core), panel: 2 (over x).
Axes of the slice: x: 2, y: 2, z: 4, core: 2. Of those that a mesh axis runs over, the one named last changes fastest.
Arguments:
- orbit_angles: float32 [2, 8192], P(None, ('groups', 'tm')), parts along dimension 1, may hold values from -3.15 to 3.15, as said below
- gap_mask: int32 [8192], P(('groups', 'tm')), parts along dimension 0, may hold values 0 or 1
- column_index: int32 [2, 512], P(None, 'panel'), may hold values from -280 to 280, as said below
- lat_coeffs: bfloat16 [2, 640, 512], P('comp', None, 'panel'), may hold values from -6 to 6
- psd_table: int32 [2, 2049], P('comp'), may hold values from 1024 to 32752, as said below
Outputs:
- normals: float32 [1024, 512], P(('groups', 'tm'), 'panel'), parts along dimension 0
There are 2 independent parts, one for each index of `groups`. A program takes and returns all parts, laid end to end along the dimension named above; an argument that names none is the same for every part. Nothing has to cross between parts.
Inputs may be any that keep to these rules, and one draw needn't show every extreme that they name: orbit_angles holds colatitude in its first row and longitude in its second. `column_index`: the first row holds each unknown's degree, the second its order; a degree is at least 2 and at least the order's magnitude; a negative order stands for the sine term in longitude. `psd_table`: entry g of a component's row is its noise power at frequency g (and 4096 - g), times 8192.
All inputs are finite; a program needn't handle non-finite values. No bound on the sum of `gap_mask` on one device may be relied on, other than what follows from the above.
Results may differ from a plain program's by a relative error of at most 0.0016.
Values may be sent and summed in bfloat16 or wider, within the bound.
No kernel may reach another device: no remote copies, remote signals or barrier semaphores. Data moves between devices by JAX's collectives and lax.ppermute only.
A program may use at most 64 MiB of HBM per device.

v0:
```python
import math
import jax
import jax.numpy as jnp
from jax import lax
from jax.sharding import PartitionSpec as P

SPLIT = 64


def synthesize(angles, keep_rows, column_index, coeffs):
    terms_lat = coeffs.shape[0] // 2
    colatitude = angles[0]
    longit = angles[1]
    wavenumbers = jnp.arange(terms_lat, dtype=jnp.float32)
    phases = colatitude[:, None] * wavenumbers[None, :]
    basis_rows = jnp.concatenate([jnp.cos(phases), jnp.sin(phases)], axis=1).astype(jnp.bfloat16)
    degree = column_index[0]
    orders = column_index[1]
    levels = jnp.arange(2 * terms_lat, dtype=jnp.int32) % terms_lat
    allowed = levels[:, None] <= degree[None, :]
    masked = jnp.where(allowed, coeffs, jnp.zeros_like(coeffs))
    latitude = jnp.dot(basis_rows, masked, preferred_element_type=jnp.float32)
    lon_phase = longit[:, None] * jnp.abs(orders).astype(jnp.float32)[None, :]
    lon_wave = jnp.where(orders[None, :] >= 0, jnp.cos(lon_phase), jnp.sin(lon_phase))
    norm_scale = 1.0 / jnp.sqrt(degree.astype(jnp.float32) + 1.0)
    return latitude * lon_wave * (keep_rows[:, None] * norm_scale[None, :])


def phase_tables(row_index, col_index, length):
    product = row_index[:, None] * col_index[None, :] % length
    angle_grid = product.astype(jnp.float32) * (2.0 * math.pi / length)
    return (jnp.cos(angle_grid), jnp.sin(angle_grid))


def dft_tables(length):
    indices = jnp.arange(length, dtype=jnp.int32)
    return phase_tables(indices, indices, length)


def rotate(real_part, imag_part, outer_index, inner_index, length):
    index_grid = outer_index[:, None] * inner_index[None, :] % length
    angle_grid = index_grid.astype(jnp.float32) * (2.0 * math.pi / length)
    cosine = jnp.cos(angle_grid)[:, :, None]
    sine_grid = jnp.sin(angle_grid)[:, :, None]
    return (real_part * cosine + imag_part * sine_grid, imag_part * cosine - real_part * sine_grid)


def precise_dot(left_side, right_side):
    return jnp.dot(
        left_side, right_side, precision=lax.Precision.HIGHEST, preferred_element_type=jnp.float32
    )


def transform(cos_table, sin_table, real_part, imag_part):
    new_real = precise_dot(cos_table, real_part) + precise_dot(sin_table, imag_part)
    new_imag = precise_dot(cos_table, imag_part) - precise_dot(sin_table, real_part)
    return (new_real, new_imag)


def four_step(real_in, imag_in, samples):
    length = real_in.shape[0]
    columns = real_in.shape[1]
    outer_count = SPLIT
    inner_count = length // SPLIT
    real_part = real_in.reshape(outer_count, inner_count * columns)
    imag_part = imag_in.reshape(outer_count, inner_count * columns)
    cos_outer, sin_outer = dft_tables(outer_count)
    real_part, imag_part = transform(cos_outer, sin_outer, real_part, imag_part)
    real_part = real_part.reshape(outer_count, inner_count, columns)
    imag_part = imag_part.reshape(outer_count, inner_count, columns)
    real_part, imag_part = rotate(
        real_part,
        imag_part,
        jnp.arange(outer_count, dtype=jnp.int32),
        jnp.arange(inner_count, dtype=jnp.int32),
        length,
    )
    real_part = jnp.transpose(real_part, (1, 0, 2)).reshape(inner_count, outer_count * columns)
    imag_part = jnp.transpose(imag_part, (1, 0, 2)).reshape(inner_count, outer_count * columns)
    cos_inner, sin_inner = dft_tables(inner_count)
    real_part, imag_part = transform(cos_inner, sin_inner, real_part, imag_part)
    return (
        real_part.reshape(length, columns) / samples,
        imag_part.reshape(length, columns) / samples,
    )


def local_transform(received, samples):
    real_part, imag_part = four_step(received[0, 0], received[1, 0], samples)
    return (real_part.astype(jnp.bfloat16), imag_part.astype(jnp.bfloat16))


def noise_weighted(spectra, psd_row, frequency, samples):
    folded = jnp.minimum(frequency, samples - frequency)
    inverse_psd = 8192.0 / jnp.take(psd_row, folded).astype(jnp.float32)
    return (spectra.astype(jnp.float32) * inverse_psd[None, :, None]).astype(jnp.bfloat16)


def settle(partial_value, sum_dim):
    summed = lax.psum_scatter(partial_value, "tm", scatter_dimension=sum_dim, tiled=True)
    return lax.psum(summed, "comp")


def body(orbit_angles, gap_mask, column_index, lat_coeffs, psd_table):
    devices_tm = lax.axis_size("tm")
    epochs = orbit_angles.shape[1]
    block_len = epochs // devices_tm
    samples = epochs * devices_tm
    columns = lat_coeffs.shape[2]
    coeffs = lat_coeffs[0]
    keep_rows = gap_mask.astype(jnp.float32)
    packed = jnp.concatenate([orbit_angles, keep_rows[None]], axis=0)[:, None, :]
    received = lax.all_to_all(packed, "tm", split_axis=2, concat_axis=1, tiled=True)
    flat_orbit = received.reshape(3, devices_tm * block_len)
    spread = synthesize(flat_orbit[0:2], flat_orbit[2], column_index, coeffs).reshape(
        devices_tm, block_len, columns
    )
    position = lax.axis_index("tm")
    local_epoch = position * block_len + jnp.arange(block_len, dtype=jnp.int32)
    cos_outer, sin_outer = dft_tables(devices_tm)
    flat_design = spread.reshape(devices_tm, block_len * columns)
    real_part = precise_dot(cos_outer, flat_design).reshape(devices_tm, block_len, columns)
    imag_part = -precise_dot(sin_outer, flat_design).reshape(devices_tm, block_len, columns)
    real_part, imag_part = rotate(
        real_part, imag_part, jnp.arange(devices_tm, dtype=jnp.int32), local_epoch, samples
    )
    twisted = jnp.stack([real_part, imag_part])
    spec_real, spec_imag = local_transform(
        lax.all_to_all(twisted, "tm", split_axis=1, concat_axis=2, tiled=True), samples
    )
    spectra = jnp.stack([spec_real, spec_imag])
    psd_row = psd_table[0]
    contract = (((0, 1), (0, 1)), ((), ()))
    frequency = position + devices_tm * jnp.arange(epochs, dtype=jnp.int32)
    weighted = noise_weighted(spectra, psd_row, frequency, samples)
    partial_value = lax.dot_general(
        lax.all_gather(spectra, "panel", axis=2, tiled=True),
        weighted,
        contract,
        preferred_element_type=jnp.float32,
    )
    return settle(partial_value, 0)


def solution(mesh):
    return jax.shard_map(
        body,
        mesh=mesh,
        in_specs=(
            P(None, ("groups", "tm")),
            P(("groups", "tm")),
            P(None, "panel"),
            P("comp", None, "panel"),
            P("comp", None),
        ),
        out_specs=P(("groups", "tm"), "panel"),
        check_vma=False,
    )
```

profile of v0, /device:TPU:0, one launch (start us, length us, event | category | flops | bytes accessed | tf_op | source)
XLA Modules:
  0.0 205.0 jit_solution(10367188866137886708)
XLA Ops:
  6.5 0.0 copy-start
  6.5 0.0 copy-start.2
  6.5 0.7 convert_element_type.103
  7.3 0.7 pad_maximum_fusion.2
  8.0 0.2 copy.46
  8.2 0.6 broadcast.344
  8.8 2.0 reduce.9
  10.8 1.0 reshape.246
  11.8 0.0 copy-start.3
  11.8 6.4 %all-to-all-start = ((f32[4,1,768]{2,1,0:T(1,128)}), f32[4,1,768]{2,1,0:T(1,128)S(1)}, u32[]{:S(2)}, u32[]{:S(2)}) async-start(f32[4,1,768]{2,1,0:T(1,128)} %reshape.246), calls=%async_computation | async-start | bytes 24576 | tf_op jit(solution)/shard_map/all_to_all | solution.py:113
  18.2 0.0 copy-done.2
  18.3 0.1 fusion.69
  18.4 0.1 copy.47
  18.5 0.1 copy.48
  18.7 5.2 %all-to-all-done = f32[4,1,768]{2,1,0:T(1,128)S(1)} async-done(((f32[4,1,768]{2,1,0:T(1,128)}), f32[4,1,768]{2,1,0:T(1,128)S(1)}, u32[]{:S(2)}, u32[]{:S(2)}) %all-to-all-start) | async-done | bytes 12320 | tf_op jit(solution)/shard_map/all_to_all | solution.py:113
  23.8 0.7 reduce.10
  24.6 0.7 reshape.247
  25.3 10.4 %slice_reduce_fusion.1 = (f32[1024]{0:T(1024)S(1)}, f32[1024]{0:T(1024)S(1)}, f32[1024]{0:T(1024)S(1)}) fusion(f32[3,1,1024]{0,1,2:T(1,128)S(1)} %bitcast.77), kind=kLoop, calls=%fused_computation.36 | loop fusion | bytes 24576 | tf_op jit(solution)/shard_map/slice | solution.py:13
  35.7 6.5 %cosine_convert_fusion = (bf16[1024,320]{1,0:T(8,128)(2,1)S(1)}, bf16[1024,320]{1,0:T(8,128)(2,1)S(1)}) fusion(f32[1024]{0:T(1024)S(1)} %get-tuple-element.7), kind=kLoop, calls=%fused_computation.12 | loop fusion | flops 983040 | bytes 1314816 | tf_op jit(solution)/shard_map/convert
  42.3 0.0 copy-done.3
  42.3 4.4 %fusion.4 = f32[1024,256]{1,0:T(8,128)S(1)} fusion(bf16[1024,320]{1,0:T(8,128)(2,1)S(1)} %get-tuple-element.15, bf16[1024,320]{1,0:T(8,128)(2,1)S(1)} %get-tuple-element.14, f32[256]{0:T(256)S(1)} %bitcast.85, f32[1024]{0:T(1024)S(1)} %get-tuple-element.6, f32[256]{0:T(256)S(1)} %bitcast.87, f32[1024]{0:T(1024)S(1)} %get-tuple-element.5, ...), kind=kOutput, calls=%fused_computation.18 | convolution fusion | flops 339804160 | bytes 2701056 | tf_op jit(solution)/shard_map/dot_general | solution.py:22
  46.7 0.5 reshape_reshape.3
  47.2 1.9 convolution_negate_fusion
  49.2 2.8 %add_bitcast_fusion = (f32[1,4,256,256]{3,1,2,0:T(4,128)S(1)}, f32[1,4,256,256]{3,1,2,0:T(4,128)S(1)}) fusion(f32[4,256,256]{2,0,1:T(4,128)S(1)} %convolution_negate_fusion, f32[4,256]{0,1:T(8,128)S(1)} %copy.48, f32[4,256]{0,1:T(8,128)S(1)} %copy.47, f32[256,256,4]{1,2,0:T(4,128)S(1)} %bitcast.72), kind=kOutput, calls=%fused_computation.33 | convolution fusion | flops 14156000 | bytes 4202496 | tf_op jit(solution)/shard_map/dot_general | solution.py:49
  52.0 0.5 pad_maximum_fusion
  52.4 1.7 copy.49
  54.2 3.6 %all-to-all-start.1 = ((f32[2,4,256,256]{3,2,0,1:T(8,128)}), f32[2,4,256,256]{3,2,0,1:T(8,128)S(1)}, u32[]{:S(2)}, u32[]{:S(2)}) async-start(f32[2,4,256,256]{3,2,0,1:T(8,128)} %copy.49), calls=%async_computation.1 | async-start | bytes 4194304 | tf_op jit(solution)/shard_map/all_to_all | solution.py:129
  57.8 0.3 all-gather.2.cloned.1.call-start
  58.1 0.1 fusion.47
  58.1 46.7 %all-to-all-done.1 = f32[2,4,256,256]{3,2,0,1:T(8,128)S(1)} async-done(((f32[2,4,256,256]{3,2,0,1:T(8,128)}), f32[2,4,256,256]{3,2,0,1:T(8,128)S(1)}, u32[]{:S(2)}, u32[]{:S(2)}) %all-to-all-start.1) | async-done | bytes 2097184 | tf_op jit(solution)/shard_map/all_to_all | solution.py:129
  104.8 1.1 fusion.115
  105.9 0.2 reshape_squeeze.6
  106.1 1.2 fusion.26
  107.3 1.4 reshape_squeeze.7
  108.7 1.2 fusion.24
  109.9 1.2 convolution_add_fusion.1
  111.1 1.2 convolution_subtract_fusion.1
  112.3 0.3 fusion.9
  112.6 0.6 copy.60
  113.3 1.0 fusion.55
  114.3 0.6 copy.61
  114.9 1.0 fusion.53
  116.0 1.1 fusion.2
  117.1 0.2 convert_element_type.109
  117.3 1.0 copy.54
  118.3 0.0 copy-start.1
  118.3 1.1 fusion.3
  119.5 0.2 convert_element_type.111
  119.7 0.2 copy.55
  119.9 0.0 copy-done.1
  119.9 1.1 pad_maximum_fusion.1
  121.0 0.0 all-gather.2.cloned.1.call-update
  121.0 0.0 reduce-scatter.2.cloned.1.call-start
  121.1 0.0 copy-done
  121.2 6.2 %gather_fusion = s32[1024]{0:T(1024)S(1)} fusion(s32[2049]{0:T(1024)S(1)} %reduce.4, s32[1024]{0:T(1024)S(1)} %broadcast_clamp_fusion), kind=kCustom, calls=%fused_computation | custom fusion | bytes 12288 | tf_op jit(solution)/shard_map/jit(_take)/gather | solution.py:95
  127.3 26.1 %all-gather.2.cloned.1.call-done = bf16[2,1024,512]{1,2,0:T(8,128)(2,1)} async-done(((bf16[2,1024,256]{1,2,0:T(8,128)(2,1)}), bf16[2,1024,512]{1,2,0:T(8,128)(2,1)}) %all-gather.2.cloned.1.call-update) | async-done | bytes 2097168 | tf_op jit(solution)/shard_map/all_gather | solution.py:137
  153.4 3.1 %convolution_bitcast_fusion = f32[512,256]{1,0:T(8,128)} fusion(bf16[2,1024,512]{1,2,0:T(8,128)(2,1)} %all-gather.2.cloned.1.call-done, f32[1024]{0:T(1024)S(1)} %convert_divide_fusion, bf16[1,1024,256]{1,2,0:T(8,128)(2,1)S(1)} %copy.55, bf16[1,1024,256]{1,2,0:T(8,128)(2,1)S(1)} %copy-done.1), kind=kOutput, calls=%fused_computation.22 | convolution fusion | flops 538968064 | bytes 3674112 | tf_op jit(solution)/shard_map/dot_general | solution.py:136
  156.6 0.0 reduce-scatter.2.cloned.1.call-update
  156.6 0.0 all-reduce.2.cloned.1.call-start
  156.6 21.8 %reduce-scatter.2.cloned.1.call-done = f32[128,256]{1,0:T(8,128)} async-done(((f32[512,256]{1,0:T(8,128)}), f32[128,256]{1,0:T(8,128)}) %reduce-scatter.2.cloned.1.call-update) | async-done | bytes 131088 | tf_op jit(solution)/shard_map/reduce_scatter | solution.py:100
  178.4 0.0 all-reduce.2.cloned.1.call-update
  178.4 18.5 %all-reduce.2.cloned.1.call-done = f32[128,256]{1,0:T(8,128)} async-done(((f32[128,256]{1,0:T(8,128)}), f32[128,256]{1,0:T(8,128)}) %all-reduce.2.cloned.1.call-update) | async-done | bytes 131088 | tf_op jit(solution)/shard_map/psum | solution.py:101
  196.9 1.6 copy.67
  (9 shorter events, 0.1 us)
Async XLA Ops:
  6.5 114.5 %copy-start = (s32[1,2049]{1,0:T(1,128)S(1)}, s32[1,2049]{1,0:T(1,128)}, u32[]{:S(2)}) copy-start(s32[1,2049]{1,0:T(1,128)} %param.9) | copy-start | bytes 24592
  6.5 11.7 %copy-start.2 = (s32[2,256]{1,0:T(2,128)S(1)}, s32[2,256]{1,0:T(2,128)}, u32[]{:S(2)}) copy-start(s32[2,256]{1,0:T(2,128)} %param.7) | copy-start | bytes 6148
  11.8 30.5 %copy-start.3 = (bf16[1,640,256]{2,1,0:T(8,128)(2,1)S(1)}, bf16[1,640,256]{2,1,0:T(8,128)(2,1)}, u32[]{:S(2)}) copy-start(bf16[1,640,256]{2,1,0:T(8,128)(2,1)} %param.8) | copy-start | bytes 983044
  11.8 12.1 %all-to-all-start = ((f32[4,1,768]{2,1,0:T(1,128)}), f32[4,1,768]{2,1,0:T(1,128)S(1)}, u32[]{:S(2)}, u32[]{:S(2)}) async-start(f32[4,1,768]{2,1,0:T(1,128)} %reshape.246), calls=%async_computation | async-start | bytes 24576 | tf_op jit(solution)/shard_map/all_to_all | solution.py:113
  54.2 50.6 %all-to-all-start.1 = ((f32[2,4,256,256]{3,2,0,1:T(8,128)}), f32[2,4,256,256]{3,2,0,1:T(8,128)S(1)}, u32[]{:S(2)}, u32[]{:S(2)}) async-start(f32[2,4,256,256]{3,2,0,1:T(8,128)} %copy.49), calls=%async_computation.1 | async-start | bytes 4194304 | tf_op jit(solution)/shard_map/all_to_all | solution.py:129
  57.8 95.6 %all-gather.2.cloned.1.call-start = ((), (), s32[]{:S(2)}) async-start(), calls=%async_computation.3 | async-start | bytes 3145728 | tf_op jit(solution)/shard_map/all_gather | solution.py:137
  118.3 1.6 copy-start.1
  121.0 57.4 %reduce-scatter.2.cloned.1.call-start = ((), (), s32[]{:S(2)}) async-start(), calls=%async_computation.4 | async-start | bytes 655360 | tf_op jit(solution)/shard_map/reduce_scatter | solution.py:100
  156.6 40.3 %all-reduce.2.cloned.1.call-start = ((), (), s32[]{:S(2)}) async-start(), calls=%async_computation.5 | async-start | bytes 262144 | tf_op jit(solution)/shard_map/psum | solution.py:101
Sparse Core Ops, SparseCore 0:
  121.1 32.2 all-gather.1
  156.7 21.6 reduce-scatter.1
  180.7 16.1 all-reduce.1
where the time goes:
time: 205 us
  waiting for transfers between devices  118 us (58%)
  local copies, waits for them, and re-layouts  28.8 us (14%)
  matrix products  21.3 us (10%)
  between operations  13.4 us (7%)
  other arithmetic  12.8 us (6%)
  starting transfers between devices  10.4 us (5%)
    all_to_all x1, waiting for transfers between devices, body(): lax.all_to_all(twisted, 'tm', split_axis=1, concat_axis=2, tiled=True)  46.7 us
    all_gather x1, waiting for transfers between devices, body(): lax.all_gather(spectra, 'panel', axis=2, tiled=True)  26.1 us
    reduce_scatter x1, waiting for transfers between devices, settle(): lax.psum_scatter(partial_value, 'tm', scatter_dimension=sum_dim, tiled=True)  21.8 us
    psum x1, waiting for transfers between devices, settle(): return lax.psum(summed, 'comp')  18.5 us
    dot_general x10, matrix products, precise_dot(): jnp.dot(left_side, right_side, precision=lax.Precision.HIGHEST, preferred...  13.8 us
    slice x1, local copies, waits for them, and re-layouts, synthesize(): longit = angles[1]  10.4 us
    another operation x1, other arithmetic  6.55 us
    all_to_all x1, starting transfers between devices, body(): lax.all_to_all(packed, 'tm', split_axis=2, concat_axis=1, tiled=True)  6.45 us
  transfers between devices with their start and end apart: 5, of which 5 were waited for; matrix products, arithmetic and copies ran while one was open for 3% of the time, Pallas kernels for 0%

commit v1 on v0

--- a/solution.py
+++ b/solution.py
@@ -98,7 +98,7 @@
 
 def settle(partial_value, sum_dim):
     summed = lax.psum_scatter(partial_value, "tm", scatter_dimension=sum_dim, tiled=True)
-    return lax.psum(summed, "comp")
+    return jnp.sum(lax.all_gather(summed, "comp"), axis=0)
 
 
 def body(orbit_angles, gap_mask, column_index, lat_coeffs, psd_table):

time: 205 us -> 189 us (0.922)
  waiting for transfers between devices: 118 us -> 99.8 us
  blocking collectives: 0 us -> 2.19 us
    psum x1 -> x0, waiting for transfers between devices: 18.5 us -> none  [settle(): return lax.psum(summed, 'comp')]
    all_gather x0 -> x1, blocking collectives: none -> 2.19 us  [settle(): return jnp.sum(lax.all_gather(summed, 'comp'), axis=0)]
    unnamed x14 -> x13, local copies, waits for them, and re-layouts: 5.05 us -> 3.49 us
  transfers between devices with their start and end apart: 5 -> 4, of which waited for: 5 -> 4; matrix products, arithmetic and copies ran while one was open for 3% -> 4% of each run, Pallas kernels for 0% -> 0%
where the time goes in v1:
time: 189 us; the launch traced here: 188 us
  waiting for transfers between devices  99.8 us (53%)
  local copies, waits for them, and re-layouts  27.3 us (14%)
  matrix products  21.3 us (11%)
  between operations  13.7 us (7%)
  other arithmetic  13.5 us (7%)
  starting transfers between devices  10.4 us (6%)
  blocking collectives  2.19 us (1%)
    all_to_all x1, waiting for transfers between devices, body(): lax.all_to_all(twisted, 'tm', split_axis=1, concat_axis=2, tiled=True)  46.7 us
    all_gather x1, waiting for transfers between devices, body(): lax.all_gather(spectra, 'panel', axis=2, tiled=True)  26.1 us
    reduce_scatter x1, waiting for transfers between devices, settle(): lax.psum_scatter(partial_value, 'tm', scatter_dimension=sum_dim, tiled=True)  21.8 us
    dot_general x10, matrix products, precise_dot(): jnp.dot(left_side, right_side, precision=lax.Precision.HIGHEST, preferred...  13.8 us
    slice x1, local copies, waits for them, and re-layouts, synthesize(): longit = angles[1]  10.4 us
    another operation x1, other arithmetic  6.55 us
    all_to_all x1, starting transfers between devices, body(): lax.all_to_all(packed, 'tm', split_axis=2, concat_axis=1, tiled=True)  6.45 us
    gather x1, local copies, waits for them, and re-layouts, noise_weighted(): inverse_psd = 8192.0 / jnp.take(psd_row, folded).astype(jnp.float32)  6.15 us
  transfers between devices with their start and end apart: 4, of which 4 were waited for; matrix products, arithmetic and copies ran while one was open for 4% of the time, Pallas kernels for 0%

profile of v1, /device:TPU:0, one launch (start us, length us, event | category | flops | bytes accessed | tf_op | source)
XLA Modules:
  0.0 188.1 jit_solution(5268075955193681397)
XLA Ops:
  6.5 0.0 copy-start
  6.5 0.0 copy-start.2
  6.5 0.7 convert_element_type.103
  7.3 0.7 pad_maximum_fusion.2
  8.0 0.2 copy.46
  8.2 0.6 broadcast.344
  8.8 2.0 %reduce.9 = f32[1024,3]{1,0:T(8,128)S(1)} reduce(f32[1024,1,3]{2,1,0:T(1,128)S(1)} %bitcast.83, f32[]{:T(128)} %broadcast.344), dimensions={1}, to_apply=%bitcast.57.reduce_sub_computation | reduce | bytes 24580
  10.8 1.0 reshape.247
  11.8 0.0 copy-start.3
  11.8 6.4 %all-to-all-start = ((f32[4,1,768]{2,1,0:T(1,128)}), f32[4,1,768]{2,1,0:T(1,128)S(1)}, u32[]{:S(2)}, u32[]{:S(2)}) async-start(f32[4,1,768]{2,1,0:T(1,128)} %reshape.247), calls=%async_computation | async-start | bytes 24576 | tf_op jit(solution)/shard_map/all_to_all | solution.py:113
  18.2 0.0 copy-done.2
  18.3 0.1 fusion.69
  18.4 0.1 copy.47
  18.5 0.1 copy.48
  18.7 5.2 %all-to-all-done = f32[4,1,768]{2,1,0:T(1,128)S(1)} async-done(((f32[4,1,768]{2,1,0:T(1,128)}), f32[4,1,768]{2,1,0:T(1,128)S(1)}, u32[]{:S(2)}, u32[]{:S(2)}) %all-to-all-start) | async-done | bytes 12320 | tf_op jit(solution)/shard_map/all_to_all | solution.py:113
  23.8 0.7 reduce.10
  24.6 0.7 reshape.248
  25.3 10.4 %slice_reduce_fusion.1 = (f32[1024]{0:T(1024)S(1)}, f32[1024]{0:T(1024)S(1)}, f32[1024]{0:T(1024)S(1)}) fusion(f32[3,1,1024]{0,1,2:T(1,128)S(1)} %bitcast.78), kind=kLoop, calls=%fused_computation.36 | loop fusion | bytes 24576 | tf_op jit(solution)/shard_map/slice | solution.py:13
  35.7 6.5 %cosine_convert_fusion = (bf16[1024,320]{1,0:T(8,128)(2,1)S(1)}, bf16[1024,320]{1,0:T(8,128)(2,1)S(1)}) fusion(f32[1024]{0:T(1024)S(1)} %get-tuple-element.7), kind=kLoop, calls=%fused_computation.12 | loop fusion | flops 983040 | bytes 1314816 | tf_op jit(solution)/shard_map/convert
  42.3 0.0 copy-done.3
  42.3 4.4 %fusion.4 = f32[1024,256]{1,0:T(8,128)S(1)} fusion(bf16[1024,320]{1,0:T(8,128)(2,1)S(1)} %get-tuple-element.15, bf16[1024,320]{1,0:T(8,128)(2,1)S(1)} %get-tuple-element.14, f32[256]{0:T(256)S(1)} %bitcast.87, f32[1024]{0:T(1024)S(1)} %get-tuple-element.6, f32[256]{0:T(256)S(1)} %bitcast.89, f32[1024]{0:T(1024)S(1)} %get-tuple-element.5, ...), kind=kOutput, calls=%fused_computation.18 | convolution fusion | flops 339804160 | bytes 2701056 | tf_op jit(solution)/shard_map/dot_general | solution.py:22
  46.7 0.5 reshape_reshape.3
  47.2 1.9 %convolution_negate_fusion = f32[4,256,256]{2,0,1:T(4,128)S(1)} fusion(f32[256,256,4]{1,2,0:T(4,128)S(1)} %bitcast.72), kind=kOutput, calls=%fused_computation.16 | convolution fusion | flops 12845280 | bytes 2097152 | tf_op jit(solution)/shard_map/dot_general | solution.py:49
  49.2 2.8 %add_bitcast_fusion = (f32[1,4,256,256]{3,1,2,0:T(4,128)S(1)}, f32[1,4,256,256]{3,1,2,0:T(4,128)S(1)}) fusion(f32[4,256,256]{2,0,1:T(4,128)S(1)} %convolution_negate_fusion, f32[4,256]{0,1:T(8,128)S(1)} %copy.48, f32[4,256]{0,1:T(8,128)S(1)} %copy.47, f32[256,256,4]{1,2,0:T(4,128)S(1)} %bitcast.73), kind=kOutput, calls=%fused_computation.33 | convolution fusion | flops 14156000 | bytes 4202496 | tf_op jit(solution)/shard_map/dot_general | solution.py:49
  52.0 0.5 pad_maximum_fusion
  52.4 1.7 copy.49
  54.2 3.6 %all-to-all-start.1 = ((f32[2,4,256,256]{3,2,0,1:T(8,128)}), f32[2,4,256,256]{3,2,0,1:T(8,128)S(1)}, u32[]{:S(2)}, u32[]{:S(2)}) async-start(f32[2,4,256,256]{3,2,0,1:T(8,128)} %copy.49), calls=%async_computation.1 | async-start | bytes 4194304 | tf_op jit(solution)/shard_map/all_to_all | solution.py:129
  57.8 0.3 all-gather.3.cloned.1.call-start
  58.1 0.1 fusion.47
  58.1 46.7 %all-to-all-done.1 = f32[2,4,256,256]{3,2,0,1:T(8,128)S(1)} async-done(((f32[2,4,256,256]{3,2,0,1:T(8,128)}), f32[2,4,256,256]{3,2,0,1:T(8,128)S(1)}, u32[]{:S(2)}, u32[]{:S(2)}) %all-to-all-start.1) | async-done | bytes 2097184 | tf_op jit(solution)/shard_map/all_to_all | solution.py:129
  104.8 1.1 fusion.115
  105.9 0.2 reshape_squeeze.6
  106.1 1.2 fusion.26
  107.3 1.4 reshape_squeeze.7
  108.7 1.2 fusion.24
  109.9 1.2 convolution_add_fusion.1
  111.1 1.2 convolution_subtract_fusion.1
  112.3 0.3 fusion.9
  112.6 0.6 copy.60
  113.3 1.0 fusion.55
  114.3 0.6 copy.61
  114.9 1.0 fusion.53
  116.0 1.1 fusion.2
  117.1 0.2 convert_element_type.109
  117.3 1.0 copy.54
  118.3 0.0 copy-start.1
  118.3 1.1 fusion.3
  119.5 0.2 convert_element_type.111
  119.7 0.2 copy.55
  119.9 0.0 copy-done.1
  119.9 1.1 pad_maximum_fusion.1
  121.0 0.0 all-gather.3.cloned.1.call-update
  121.0 0.0 reduce-scatter.2.cloned.1.call-start
  121.1 0.0 copy-done
  121.2 6.2 %gather_fusion = s32[1024]{0:T(1024)S(1)} fusion(s32[2049]{0:T(1024)S(1)} %reduce.4, s32[1024]{0:T(1024)S(1)} %broadcast_clamp_fusion), kind=kCustom, calls=%fused_computation | custom fusion | bytes 12288 | tf_op jit(solution)/shard_map/jit(_take)/gather | solution.py:95
  127.3 26.1 %all-gather.3.cloned.1.call-done = bf16[2,1024,512]{1,2,0:T(8,128)(2,1)} async-done(((bf16[2,1024,256]{1,2,0:T(8,128)(2,1)}), bf16[2,1024,512]{1,2,0:T(8,128)(2,1)}) %all-gather.3.cloned.1.call-update) | async-done | bytes 2097168 | tf_op jit(solution)/shard_map/all_gather | solution.py:137
  153.4 3.1 %convolution_bitcast_fusion = f32[512,256]{1,0:T(8,128)} fusion(bf16[2,1024,512]{1,2,0:T(8,128)(2,1)} %all-gather.3.cloned.1.call-done, f32[1024]{0:T(1024)S(1)} %convert_divide_fusion, bf16[1,1024,256]{1,2,0:T(8,128)(2,1)S(1)} %copy.55, bf16[1,1024,256]{1,2,0:T(8,128)(2,1)S(1)} %copy-done.1), kind=kOutput, calls=%fused_computation.22 | convolution fusion | flops 538968064 | bytes 3674112 | tf_op jit(solution)/shard_map/dot_general | solution.py:136
  156.6 0.0 reduce-scatter.2.cloned.1.call-update
  156.6 21.8 %reduce-scatter.2.cloned.1.call-done = f32[128,256]{1,0:T(8,128)} async-done(((f32[512,256]{1,0:T(8,128)}), f32[128,256]{1,0:T(8,128)}) %reduce-scatter.2.cloned.1.call-update) | async-done | bytes 131088 | tf_op jit(solution)/shard_map/reduce_scatter | solution.py:100
  178.4 2.2 %all-gather = f32[256,256]{1,0:T(8,128)S(1)} all-gather(f32[128,256]{1,0:T(8,128)} %reduce-scatter.2.cloned.1.call-done), channel_id=2, replica_groups=mesh['groups'=2,'tm'=4,'comp'=2,'panel'=2] {'comp'}, dimensions={0}, use_global_device_ids=true | all-gather | bytes 393216 | tf_op jit(solution)/shard_map/all_gather | solution.py:101
  180.6 0.7 reduce_sum.9
  (9 shorter events, 0.1 us)
Async XLA Ops:
  6.5 114.5 %copy-start = (s32[1,2049]{1,0:T(1,128)S(1)}, s32[1,2049]{1,0:T(1,128)}, u32[]{:S(2)}) copy-start(s32[1,2049]{1,0:T(1,128)} %param.9) | copy-start | bytes 24592
  6.5 11.7 %copy-start.2 = (s32[2,256]{1,0:T(2,128)S(1)}, s32[2,256]{1,0:T(2,128)}, u32[]{:S(2)}) copy-start(s32[2,256]{1,0:T(2,128)} %param.7) | copy-start | bytes 6148
  11.8 30.5 %copy-start.3 = (bf16[1,640,256]{2,1,0:T(8,128)(2,1)S(1)}, bf16[1,640,256]{2,1,0:T(8,128)(2,1)}, u32[]{:S(2)}) copy-start(bf16[1,640,256]{2,1,0:T(8,128)(2,1)} %param.8) | copy-start | bytes 983044
  11.8 12.1 %all-to-all-start = ((f32[4,1,768]{2,1,0:T(1,128)}), f32[4,1,768]{2,1,0:T(1,128)S(1)}, u32[]{:S(2)}, u32[]{:S(2)}) async-start(f32[4,1,768]{2,1,0:T(1,128)} %reshape.247), calls=%async_computation | async-start | bytes 24576 | tf_op jit(solution)/shard_map/all_to_all | solution.py:113
  54.2 50.6 %all-to-all-start.1 = ((f32[2,4,256,256]{3,2,0,1:T(8,128)}), f32[2,4,256,256]{3,2,0,1:T(8,128)S(1)}, u32[]{:S(2)}, u32[]{:S(2)}) async-start(f32[2,4,256,256]{3,2,0,1:T(8,128)} %copy.49), calls=%async_computation.1 | async-start | bytes 4194304 | tf_op jit(solution)/shard_map/all_to_all | solution.py:129
  57.8 95.6 %all-gather.3.cloned.1.call-start = ((), (), s32[]{:S(2)}) async-start(), calls=%async_computation.3 | async-start | bytes 3145728 | tf_op jit(solution)/shard_map/all_gather | solution.py:137
  118.3 1.6 copy-start.1
  121.0 57.4 %reduce-scatter.2.cloned.1.call-start = ((), (), s32[]{:S(2)}) async-start(), calls=%async_computation.4 | async-start | bytes 655360 | tf_op jit(solution)/shard_map/reduce_scatter | solution.py:100
Sparse Core Ops, SparseCore 0:
  121.1 32.2 all-gather.2
  156.7 21.6 reduce-scatter.1
